TPU v7x, 128 devices: a whole 4x4x4 slice. The times are simulated.
128 devices in a mesh: gx: 8 (over z, core), gy: 16 (over y, x).
Axes of the slice: x: 4, y: 4, z: 4, core: 2. Of those that a mesh axis runs over, the one named last changes fastest.
Arguments:
- hidden_in: bfloat16 [32768, 3584], P(('gx', 'gy')), may hold values from -6 to 6
- lengths: int32 [8, 4], P('gx'), may hold values from 1 to 2048, 4096 in all within a row
- attn_norm: float32 [3584], replicated, may hold values from 0.5 to 1.5
- qkv_weight: bfloat16 [3584, 4608], P('gx', 'gy'), may hold values from -0.09375 to 0.09375
- qkv_bias: float32 [4608], replicated, may hold values from -5 to 5
Outputs:
- attn: bfloat16 [32768, 3584], P(('gx', 'gy'))
- kv_rows: bfloat16 [32768, 1024], P(('gx', 'gy'))
Inputs may be any that keep to these rules, and one draw needn't show every extreme that they name: Each row of lengths sums to 4096; the longest of each row is exactly 2048.
All inputs are finite; a program needn't handle non-finite values.
Results may differ from a plain program's by a relative error of at most 0.0035.
The roundings to bfloat16 on the way count: a program that leaves them out, or rounds other values in their place, can miss the bound.
Values may be sent and summed in bfloat16 or wider, within the bound.
No kernel may reach another device: no remote copies, remote signals or barrier semaphores. Data moves between devices by JAX's collectives and lax.ppermute only.
A program may use at most 128 MiB of HBM per device.

v0:
```python
import math
import jax
import jax.numpy as jnp
from jax import lax
from jax.sharding import PartitionSpec as P

HEADS = 28
KV_HEADS = 4
HEAD_DIM = 128
key_span = 512


def norm_rows(values, gain):
    wide = values.astype(jnp.float32)
    scale = lax.rsqrt(jnp.mean(wide * wide, axis=1, keepdims=True) + 1e-06)
    return (wide * scale * gain[None, :]).astype(jnp.bfloat16)


def segment_of(index, ends):
    return jnp.sum((ends[None, :] <= index[:, None]).astype(jnp.int32), axis=1)


def rotate(block, pos, heads):
    half = HEAD_DIM // 2
    freqs = 1000000.0 ** (-2.0 * jnp.arange(half, dtype=jnp.float32) / HEAD_DIM)
    angle = pos.astype(jnp.float32)[:, None, None] * freqs[None, None, :]
    wide = block.astype(jnp.float32).reshape(block.shape[0], heads, HEAD_DIM)
    first, second = (wide[..., :half], wide[..., half:])
    turned = jnp.concatenate(
        [
            first * jnp.cos(angle) - second * jnp.sin(angle),
            second * jnp.cos(angle) + first * jnp.sin(angle),
        ],
        axis=2,
    )
    return turned.reshape(block.shape[0], heads * HEAD_DIM).astype(jnp.bfloat16)


def project_joined(normed, weight, bias):
    grouped = lax.all_gather(normed, "gy", axis=0, tiled=True)
    summed = jnp.dot(
        grouped,
        lax.all_gather(weight, "gx", axis=0, tiled=True),
        preferred_element_type=jnp.float32,
    )
    width = weight.shape[1]
    bias_block = lax.dynamic_slice_in_dim(bias, lax.axis_index("gy") * width, width, 0)
    block_out = (summed + bias_block[None, :]).astype(jnp.bfloat16)
    return lax.all_to_all(block_out, "gy", split_axis=0, concat_axis=1, tiled=True)


def on_device(hidden_in, lengths, attn_norm, qkv_weight, qkv_bias):
    rows = hidden_in.shape[0]
    first = lax.axis_index("gy") * rows
    row_lengths = lengths[0]
    qdim = HEADS * HEAD_DIM
    kdim = KV_HEADS * HEAD_DIM
    group = HEADS // KV_HEADS
    normed = norm_rows(hidden_in, attn_norm)
    joined = project_joined(normed, qkv_weight, qkv_bias)
    ends = jnp.cumsum(row_lengths)
    tokens_here = first + jnp.arange(rows, dtype=jnp.int32)
    before = ends[None, :] <= tokens_here[:, None]
    seg_here = jnp.sum(before.astype(jnp.int32), axis=1)
    begin = jnp.sum(jnp.where(before, row_lengths[None, :], 0), axis=1)
    pos = tokens_here - begin
    queries = rotate(joined[:, :qdim], pos, HEADS).reshape(rows, KV_HEADS, group, HEAD_DIM)
    keys = rotate(joined[:, qdim : qdim + kdim], pos, KV_HEADS)
    kv_rows = jnp.concatenate([keys, joined[:, qdim + kdim :]], axis=1)
    scale = 1.0 / HEAD_DIM**0.5

    def attend(carry, piece, start):
        running, total, summed = carry
        key_count = piece.shape[0]
        key_index = start + jnp.arange(key_count, dtype=jnp.int32)
        key_seg = segment_of(key_index, ends)
        key_part = piece[:, :kdim].reshape(key_count, KV_HEADS, HEAD_DIM)
        value_part = piece[:, kdim:].reshape(key_count, KV_HEADS, HEAD_DIM)
        scores = (
            jnp.einsum("rgho,ngo->ghrn", queries, key_part, preferred_element_type=jnp.float32)
            * scale
        )
        allowed = (seg_here[:, None] == key_seg[None, :]) & (
            key_index[None, :] <= tokens_here[:, None]
        )
        newest = jnp.maximum(running, jnp.max(jnp.where(allowed, scores, -1e30), axis=3))
        shrink = jnp.exp(running - newest)
        weights = jnp.where(allowed, jnp.exp(scores - newest[..., None]), 0.0)
        total = total * shrink + jnp.sum(weights, axis=3)
        summed = summed * shrink[..., None] + jnp.einsum(
            "ghrn,ngo->ghro",
            weights.astype(jnp.bfloat16),
            value_part,
            preferred_element_type=jnp.float32,
        )
        return (newest, total, summed)

    def visit(carry, piece, start):
        return attend(carry, piece, start)

    start_state = (
        jnp.full((KV_HEADS, group, rows), -1e30, jnp.float32),
        jnp.zeros((KV_HEADS, group, rows), jnp.float32),
        jnp.zeros((KV_HEADS, group, rows, HEAD_DIM), jnp.float32),
    )
    piece = lax.all_gather(kv_rows, "gy", axis=0, tiled=True)
    length = piece.shape[0]
    span = math.gcd(length, key_span)
    stacked = piece.reshape(length // span, span, piece.shape[1])
    offsets = jnp.arange(length // span, dtype=jnp.int32) * span

    def advance(state, item):
        return (visit(state, item[0], item[1]), None)

    final_state, unused = lax.scan(advance, start_state, (stacked, offsets))
    running, total, summed = final_state
    attn = (
        jnp.transpose(summed / total[..., None], (2, 0, 1, 3))
        .reshape(rows, qdim)
        .astype(jnp.bfloat16)
    )
    return (attn, kv_rows)


def solution(mesh):
    placed = (P(("gx", "gy"), None), P("gx", None), P(), P("gx", "gy"), P())
    return jax.shard_map(
        on_device,
        mesh=mesh,
        in_specs=placed,
        out_specs=(P(("gx", "gy"), None), P(("gx", "gy"), None)),
        check_vma=False,
    )
```

profile of v0, /device:TPU:0, one launch (start us, length us, event | category | flops | bytes accessed | tf_op | source)
XLA Modules:
  0.0 595.3 jit_solution(592481126304964280)
XLA Ops:
  13.9 24.0 %all-gather.9.cloned.1.call-done = bf16[8,448,288]{1,2,0:T(8,128)(2,1)} async-done(((bf16[1,448,288]{1,2,0:T(8,128)(2,1)}), bf16[8,448,288]{1,2,0:T(8,128)(2,1)}) %all-gather.9.cloned.1.call-update) | async-done | bytes 2064400 | tf_op jit(solution)/shard_map/all_gather | solution.py:43
  44.5 172.0 %all-gather.5.cloned.1.call-done = bf16[4096,3584]{1,0:T(8,128)(2,1)} async-done(((bf16[256,3584]{1,0:T(8,128)(2,1)}), bf16[4096,3584]{1,0:T(8,128)(2,1)}) %all-gather.5.cloned.1.call-update) | async-done | bytes 29360144 | tf_op jit(solution)/shard_map/all_gather | solution.py:40
  216.6 14.7 %fusion.16 = bf16[4096,288]{0,1:T(8,128)(2,1)S(1)} fusion(bf16[4096,3584]{1,0:T(8,128)(2,1)} %all-gather.5.cloned.1.call-done, bf16[3584,288]{0,1:T(8,128)(2,1)} %reshape.172, f32[288]{0:T(512)S(1)} %dynamic_slice.11), kind=kOutput, calls=%fused_computation.25 | convolution fusion | flops 8458076160 | bytes 33784960 | tf_op jit(solution)/shard_map/dot_general | solution.py:41
  233.0 5.3 all-to-all-start
  239.1 34.4 %all-to-all-done = bf16[16,256,288]{1,2,0:T(8,128)(2,1)S(1)} async-done(((bf16[16,256,288]{1,2,0:T(8,128)(2,1)}), bf16[16,256,288]{1,2,0:T(8,128)(2,1)S(1)}, u32[]{:S(2)}, u32[]{:S(2)}) %all-to-all-start) | async-done | bytes 2359328 | tf_op jit(solution)/shard_map/all_to_all | solution.py:49
  283.8 65.9 %all-gather.7.cloned.1.call-done = bf16[4096,1024]{0,1:T(8,128)(2,1)} async-done(((bf16[256,1024]{0,1:T(8,128)(2,1)}), bf16[4096,1024]{0,1:T(8,128)(2,1)}) %all-gather.7.cloned.1.call-update) | async-done | bytes 8388624 | tf_op jit(solution)/shard_map/all_gather | solution.py:106
  349.7 7.5 %copy.52 = bf16[128,8,8,512]{3,2,0,1:T(8,128)(2,1)} copy(bf16[128,8,8,512]{3,2,1,0:T(8,128)(2,1)} %bitcast.86) | data formatting | bytes 16777216 | tf_op jit(solution)/shard_map/reshape | solution.py:109
  357.2 222.0 %while.15 = (s32[]{:T(128)}, f32[4,7,256]{2,1,0:T(8,128)S(1)}, f32[4,7,256]{2,1,0:T(8,128)S(1)}, f32[4,7,256,128]{3,2,1,0:T(8,128)}, s32[256]{0:T(256)S(1)}, /*i...) while((s32[]{:T(128)}, f32[4,7,256]{2,1,0:T(8,128)S(1)}, ...), condition=%wide.region_8.9_spmd.clone, body=%wide.region_4.8_spmd.clone.sunk | while | flops 1922606336 | bytes 88814816 | solution.py:115
  360.1 6.5 %fusion.43 = (f32[4,7,256]{2,1,0:T(8,128)S(1)}, f32[4,512,256,7]{2,1,3,0:T(8,128)}) fusion(pred[256,512]{0,1:T(8,128)(4,1)S(1)} %compare_and_fusion.2, bf16[512,4,128,1]{0,2,3,1:T(8,128)(2,1)S(1)} %bitcast.80, bf16[256,4,7,128]{3,0,2,1:T(8,128)(2,1)S(1)} %get-tuple-element.270), kind=kOutput, calls=%fused_computation.3.clone.1 | convolution fusion | flops 950526976 | bytes 17199104 | tf_op jit(solution)/shard_map/while/body/eval_jaxpr/rgho,ngo->ghrn/dot_general | solution.py:80
  366.6 8.3 %fusion.44 = f32[4,7,256]{2,1,0:T(8,128)S(1)} fusion(f32[4,512,256,7]{2,1,3,0:T(8,128)} %get-tuple-element.234, f32[4,7,256]{2,1,0:T(8,128)S(1)} %select_maximum_fusion.2, pred[256,512]{0,1:T(8,128)(4,1)S(1)} %compare_and_fusion.2), kind=kLoop, calls=%fused_computation.7.clone.1 | loop fusion | flops 14672896 | bytes 14868480 | tf_op jit(solution)/shard_map/while/body/eval_jaxpr/reduce_sum | solution.py:89
  375.0 8.0 %fusion.46 = f32[4,7,256,128]{3,2,1,0:T(8,128)S(1)} fusion(f32[4,7,256,128]{3,2,1,0:T(8,128)S(1)} %copy-done.1, bf16[512,4,128,1]{0,2,3,1:T(8,128)(2,1)S(1)} %bitcast.82, f32[4,512,256,7]{2,1,3,0:T(8,128)} %get-tuple-element.234, f32[4,7,256]{2,1,0:T(8,128)S(1)} %select_maximum_fusion.2, pred[256,512]{0,1:T(8,128)(4,1)S(1)} %compare_and_fusion.2, ...), kind=kOutput, calls=%fused_computation.11.clone.1 | convolution fusion | flops 956956672 | bytes 22732800 | tf_op jit(solution)/shard_map/while/body/eval_jaxpr/ghrn,ngo->ghro/dot_general | solution.py:90
  387.8 6.5 %fusion.43 = (f32[4,7,256]{2,1,0:T(8,128)S(1)}, f32[4,512,256,7]{2,1,3,0:T(8,128)}) fusion(pred[256,512]{0,1:T(8,128)(4,1)S(1)} %compare_and_fusion.2, bf16[512,4,128,1]{0,2,3,1:T(8,128)(2,1)S(1)} %bitcast.80, bf16[256,4,7,128]{3,0,2,1:T(8,128)(2,1)S(1)} %get-tuple-element.270), kind=kOutput, calls=%fused_computation.3.clone.1 | convolution fusion | flops 950526976 | bytes 17199104 | tf_op jit(solution)/shard_map/while/body/eval_jaxpr/rgho,ngo->ghrn/dot_general | solution.py:80
  394.4 8.3 %fusion.44 = f32[4,7,256]{2,1,0:T(8,128)S(1)} fusion(f32[4,512,256,7]{2,1,3,0:T(8,128)} %get-tuple-element.234, f32[4,7,256]{2,1,0:T(8,128)S(1)} %select_maximum_fusion.2, pred[256,512]{0,1:T(8,128)(4,1)S(1)} %compare_and_fusion.2), kind=kLoop, calls=%fused_computation.7.clone.1 | loop fusion | flops 14672896 | bytes 14868480 | tf_op jit(solution)/shard_map/while/body/eval_jaxpr/reduce_sum | solution.py:89
  402.7 8.0 %fusion.46 = f32[4,7,256,128]{3,2,1,0:T(8,128)S(1)} fusion(f32[4,7,256,128]{3,2,1,0:T(8,128)S(1)} %copy-done.1, bf16[512,4,128,1]{0,2,3,1:T(8,128)(2,1)S(1)} %bitcast.82, f32[4,512,256,7]{2,1,3,0:T(8,128)} %get-tuple-element.234, f32[4,7,256]{2,1,0:T(8,128)S(1)} %select_maximum_fusion.2, pred[256,512]{0,1:T(8,128)(4,1)S(1)} %compare_and_fusion.2, ...), kind=kOutput, calls=%fused_computation.11.clone.1 | convolution fusion | flops 956956672 | bytes 22732800 | tf_op jit(solution)/shard_map/while/body/eval_jaxpr/ghrn,ngo->ghro/dot_general | solution.py:90
  415.6 6.5 %fusion.43 = (f32[4,7,256]{2,1,0:T(8,128)S(1)}, f32[4,512,256,7]{2,1,3,0:T(8,128)}) fusion(pred[256,512]{0,1:T(8,128)(4,1)S(1)} %compare_and_fusion.2, bf16[512,4,128,1]{0,2,3,1:T(8,128)(2,1)S(1)} %bitcast.80, bf16[256,4,7,128]{3,0,2,1:T(8,128)(2,1)S(1)} %get-tuple-element.270), kind=kOutput, calls=%fused_computation.3.clone.1 | convolution fusion | flops 950526976 | bytes 17199104 | tf_op jit(solution)/shard_map/while/body/eval_jaxpr/rgho,ngo->ghrn/dot_general | solution.py:80
  422.1 8.3 %fusion.44 = f32[4,7,256]{2,1,0:T(8,128)S(1)} fusion(f32[4,512,256,7]{2,1,3,0:T(8,128)} %get-tuple-element.234, f32[4,7,256]{2,1,0:T(8,128)S(1)} %select_maximum_fusion.2, pred[256,512]{0,1:T(8,128)(4,1)S(1)} %compare_and_fusion.2), kind=kLoop, calls=%fused_computation.7.clone.1 | loop fusion | flops 14672896 | bytes 14868480 | tf_op jit(solution)/shard_map/while/body/eval_jaxpr/reduce_sum | solution.py:89
  430.5 8.0 %fusion.46 = f32[4,7,256,128]{3,2,1,0:T(8,128)S(1)} fusion(f32[4,7,256,128]{3,2,1,0:T(8,128)S(1)} %copy-done.1, bf16[512,4,128,1]{0,2,3,1:T(8,128)(2,1)S(1)} %bitcast.82, f32[4,512,256,7]{2,1,3,0:T(8,128)} %get-tuple-element.234, f32[4,7,256]{2,1,0:T(8,128)S(1)} %select_maximum_fusion.2, pred[256,512]{0,1:T(8,128)(4,1)S(1)} %compare_and_fusion.2, ...), kind=kOutput, calls=%fused_computation.11.clone.1 | convolution fusion | flops 956956672 | bytes 22732800 | tf_op jit(solution)/shard_map/while/body/eval_jaxpr/ghrn,ngo->ghro/dot_general | solution.py:90
  443.3 6.5 %fusion.43 = (f32[4,7,256]{2,1,0:T(8,128)S(1)}, f32[4,512,256,7]{2,1,3,0:T(8,128)}) fusion(pred[256,512]{0,1:T(8,128)(4,1)S(1)} %compare_and_fusion.2, bf16[512,4,128,1]{0,2,3,1:T(8,128)(2,1)S(1)} %bitcast.80, bf16[256,4,7,128]{3,0,2,1:T(8,128)(2,1)S(1)} %get-tuple-element.270), kind=kOutput, calls=%fused_computation.3.clone.1 | convolution fusion | flops 950526976 | bytes 17199104 | tf_op jit(solution)/shard_map/while/body/eval_jaxpr/rgho,ngo->ghrn/dot_general | solution.py:80
  449.9 8.3 %fusion.44 = f32[4,7,256]{2,1,0:T(8,128)S(1)} fusion(f32[4,512,256,7]{2,1,3,0:T(8,128)} %get-tuple-element.234, f32[4,7,256]{2,1,0:T(8,128)S(1)} %select_maximum_fusion.2, pred[256,512]{0,1:T(8,128)(4,1)S(1)} %compare_and_fusion.2), kind=kLoop, calls=%fused_computation.7.clone.1 | loop fusion | flops 14672896 | bytes 14868480 | tf_op jit(solution)/shard_map/while/body/eval_jaxpr/reduce_sum | solution.py:89
  458.2 8.0 %fusion.46 = f32[4,7,256,128]{3,2,1,0:T(8,128)S(1)} fusion(f32[4,7,256,128]{3,2,1,0:T(8,128)S(1)} %copy-done.1, bf16[512,4,128,1]{0,2,3,1:T(8,128)(2,1)S(1)} %bitcast.82, f32[4,512,256,7]{2,1,3,0:T(8,128)} %get-tuple-element.234, f32[4,7,256]{2,1,0:T(8,128)S(1)} %select_maximum_fusion.2, pred[256,512]{0,1:T(8,128)(4,1)S(1)} %compare_and_fusion.2, ...), kind=kOutput, calls=%fused_computation.11.clone.1 | convolution fusion | flops 956956672 | bytes 22732800 | tf_op jit(solution)/shard_map/while/body/eval_jaxpr/ghrn,ngo->ghro/dot_general | solution.py:90
  471.1 6.5 %fusion.43 = (f32[4,7,256]{2,1,0:T(8,128)S(1)}, f32[4,512,256,7]{2,1,3,0:T(8,128)}) fusion(pred[256,512]{0,1:T(8,128)(4,1)S(1)} %compare_and_fusion.2, bf16[512,4,128,1]{0,2,3,1:T(8,128)(2,1)S(1)} %bitcast.80, bf16[256,4,7,128]{3,0,2,1:T(8,128)(2,1)S(1)} %get-tuple-element.270), kind=kOutput, calls=%fused_computation.3.clone.1 | convolution fusion | flops 950526976 | bytes 17199104 | tf_op jit(solution)/shard_map/while/body/eval_jaxpr/rgho,ngo->ghrn/dot_general | solution.py:80
  477.6 8.3 %fusion.44 = f32[4,7,256]{2,1,0:T(8,128)S(1)} fusion(f32[4,512,256,7]{2,1,3,0:T(8,128)} %get-tuple-element.234, f32[4,7,256]{2,1,0:T(8,128)S(1)} %select_maximum_fusion.2, pred[256,512]{0,1:T(8,128)(4,1)S(1)} %compare_and_fusion.2), kind=kLoop, calls=%fused_computation.7.clone.1 | loop fusion | flops 14672896 | bytes 14868480 | tf_op jit(solution)/shard_map/while/body/eval_jaxpr/reduce_sum | solution.py:89
  486.0 8.0 %fusion.46 = f32[4,7,256,128]{3,2,1,0:T(8,128)S(1)} fusion(f32[4,7,256,128]{3,2,1,0:T(8,128)S(1)} %copy-done.1, bf16[512,4,128,1]{0,2,3,1:T(8,128)(2,1)S(1)} %bitcast.82, f32[4,512,256,7]{2,1,3,0:T(8,128)} %get-tuple-element.234, f32[4,7,256]{2,1,0:T(8,128)S(1)} %select_maximum_fusion.2, pred[256,512]{0,1:T(8,128)(4,1)S(1)} %compare_and_fusion.2, ...), kind=kOutput, calls=%fused_computation.11.clone.1 | convolution fusion | flops 956956672 | bytes 22732800 | tf_op jit(solution)/shard_map/while/body/eval_jaxpr/ghrn,ngo->ghro/dot_general | solution.py:90
  498.8 6.5 %fusion.43 = (f32[4,7,256]{2,1,0:T(8,128)S(1)}, f32[4,512,256,7]{2,1,3,0:T(8,128)}) fusion(pred[256,512]{0,1:T(8,128)(4,1)S(1)} %compare_and_fusion.2, bf16[512,4,128,1]{0,2,3,1:T(8,128)(2,1)S(1)} %bitcast.80, bf16[256,4,7,128]{3,0,2,1:T(8,128)(2,1)S(1)} %get-tuple-element.270), kind=kOutput, calls=%fused_computation.3.clone.1 | convolution fusion | flops 950526976 | bytes 17199104 | tf_op jit(solution)/shard_map/while/body/eval_jaxpr/rgho,ngo->ghrn/dot_general | solution.py:80
  505.4 8.3 %fusion.44 = f32[4,7,256]{2,1,0:T(8,128)S(1)} fusion(f32[4,512,256,7]{2,1,3,0:T(8,128)} %get-tuple-element.234, f32[4,7,256]{2,1,0:T(8,128)S(1)} %select_maximum_fusion.2, pred[256,512]{0,1:T(8,128)(4,1)S(1)} %compare_and_fusion.2), kind=kLoop, calls=%fused_computation.7.clone.1 | loop fusion | flops 14672896 | bytes 14868480 | tf_op jit(solution)/shard_map/while/body/eval_jaxpr/reduce_sum | solution.py:89
  513.7 8.0 %fusion.46 = f32[4,7,256,128]{3,2,1,0:T(8,128)S(1)} fusion(f32[4,7,256,128]{3,2,1,0:T(8,128)S(1)} %copy-done.1, bf16[512,4,128,1]{0,2,3,1:T(8,128)(2,1)S(1)} %bitcast.82, f32[4,512,256,7]{2,1,3,0:T(8,128)} %get-tuple-element.234, f32[4,7,256]{2,1,0:T(8,128)S(1)} %select_maximum_fusion.2, pred[256,512]{0,1:T(8,128)(4,1)S(1)} %compare_and_fusion.2, ...), kind=kOutput, calls=%fused_computation.11.clone.1 | convolution fusion | flops 956956672 | bytes 22732800 | tf_op jit(solution)/shard_map/while/body/eval_jaxpr/ghrn,ngo->ghro/dot_general | solution.py:90
  526.6 6.5 %fusion.43 = (f32[4,7,256]{2,1,0:T(8,128)S(1)}, f32[4,512,256,7]{2,1,3,0:T(8,128)}) fusion(pred[256,512]{0,1:T(8,128)(4,1)S(1)} %compare_and_fusion.2, bf16[512,4,128,1]{0,2,3,1:T(8,128)(2,1)S(1)} %bitcast.80, bf16[256,4,7,128]{3,0,2,1:T(8,128)(2,1)S(1)} %get-tuple-element.270), kind=kOutput, calls=%fused_computation.3.clone.1 | convolution fusion | flops 950526976 | bytes 17199104 | tf_op jit(solution)/shard_map/while/body/eval_jaxpr/rgho,ngo->ghrn/dot_general | solution.py:80
  533.1 8.3 %fusion.44 = f32[4,7,256]{2,1,0:T(8,128)S(1)} fusion(f32[4,512,256,7]{2,1,3,0:T(8,128)} %get-tuple-element.234, f32[4,7,256]{2,1,0:T(8,128)S(1)} %select_maximum_fusion.2, pred[256,512]{0,1:T(8,128)(4,1)S(1)} %compare_and_fusion.2), kind=kLoop, calls=%fused_computation.7.clone.1 | loop fusion | flops 14672896 | bytes 14868480 | tf_op jit(solution)/shard_map/while/body/eval_jaxpr/reduce_sum | solution.py:89
  541.5 8.0 %fusion.46 = f32[4,7,256,128]{3,2,1,0:T(8,128)S(1)} fusion(f32[4,7,256,128]{3,2,1,0:T(8,128)S(1)} %copy-done.1, bf16[512,4,128,1]{0,2,3,1:T(8,128)(2,1)S(1)} %bitcast.82, f32[4,512,256,7]{2,1,3,0:T(8,128)} %get-tuple-element.234, f32[4,7,256]{2,1,0:T(8,128)S(1)} %select_maximum_fusion.2, pred[256,512]{0,1:T(8,128)(4,1)S(1)} %compare_and_fusion.2, ...), kind=kOutput, calls=%fused_computation.11.clone.1 | convolution fusion | flops 956956672 | bytes 22732800 | tf_op jit(solution)/shard_map/while/body/eval_jaxpr/ghrn,ngo->ghro/dot_general | solution.py:90
  554.3 6.5 %fusion.43 = (f32[4,7,256]{2,1,0:T(8,128)S(1)}, f32[4,512,256,7]{2,1,3,0:T(8,128)}) fusion(pred[256,512]{0,1:T(8,128)(4,1)S(1)} %compare_and_fusion.2, bf16[512,4,128,1]{0,2,3,1:T(8,128)(2,1)S(1)} %bitcast.80, bf16[256,4,7,128]{3,0,2,1:T(8,128)(2,1)S(1)} %get-tuple-element.270), kind=kOutput, calls=%fused_computation.3.clone.1 | convolution fusion | flops 950526976 | bytes 17199104 | tf_op jit(solution)/shard_map/while/body/eval_jaxpr/rgho,ngo->ghrn/dot_general | solution.py:80
  560.9 8.3 %fusion.44 = f32[4,7,256]{2,1,0:T(8,128)S(1)} fusion(f32[4,512,256,7]{2,1,3,0:T(8,128)} %get-tuple-element.234, f32[4,7,256]{2,1,0:T(8,128)S(1)} %select_maximum_fusion.2, pred[256,512]{0,1:T(8,128)(4,1)S(1)} %compare_and_fusion.2), kind=kLoop, calls=%fused_computation.7.clone.1 | loop fusion | flops 14672896 | bytes 14868480 | tf_op jit(solution)/shard_map/while/body/eval_jaxpr/reduce_sum | solution.py:89
  569.2 8.0 %fusion.46 = f32[4,7,256,128]{3,2,1,0:T(8,128)S(1)} fusion(f32[4,7,256,128]{3,2,1,0:T(8,128)S(1)} %copy-done.1, bf16[512,4,128,1]{0,2,3,1:T(8,128)(2,1)S(1)} %bitcast.82, f32[4,512,256,7]{2,1,3,0:T(8,128)} %get-tuple-element.234, f32[4,7,256]{2,1,0:T(8,128)S(1)} %select_maximum_fusion.2, pred[256,512]{0,1:T(8,128)(4,1)S(1)} %compare_and_fusion.2, ...), kind=kOutput, calls=%fused_computation.11.clone.1 | convolution fusion | flops 956956672 | bytes 22732800 | tf_op jit(solution)/shard_map/while/body/eval_jaxpr/ghrn,ngo->ghro/dot_general | solution.py:90
  (153 shorter events, 74.2 us)
Async XLA Ops:
  7.2 30.8 %all-gather.9.cloned.1.call-start = ((), (), s32[]{:S(2)}) async-start(), calls=%async_computation.3 | async-start | bytes 2654208 | tf_op jit(solution)/shard_map/all_gather | solution.py:43
  7.9 208.7 %all-gather.5.cloned.1.call-start = ((), (), s32[]{:S(2)}) async-start(), calls=%async_computation.1 | async-start | bytes 31195136 | tf_op jit(solution)/shard_map/all_gather | solution.py:40
  231.3 7.2 %copy-start.3 = (s32[1,4]{1,0:T(1,128)S(1)}, s32[1,4]{1,0:T(1,128)}, u32[]{:S(2)}) copy-start(s32[1,4]{1,0:T(1,128)} %param.8) | copy-start | bytes 52
  233.0 40.5 %all-to-all-start = ((bf16[16,256,288]{1,2,0:T(8,128)(2,1)}), bf16[16,256,288]{1,2,0:T(8,128)(2,1)S(1)}, u32[]{:S(2)}, u32[]{:S(2)}) async-start(bf16[16,256,288]{1,2,0:T(8,128)(2,1)} %bitcast.85), calls=%async_computation | async-start | bytes 4718592 | tf_op jit(solution)/shard_map/all_to_all | solution.py:49
  238.2 111.5 %all-gather.7.cloned.1.call-start = ((), (), s32[]{:S(2)}) async-start(), calls=%async_computation.2 | async-start | bytes 8912896 | tf_op jit(solution)/shard_map/all_gather | solution.py:106
  274.5 1.4 copy-start
  366.6 8.4 %copy-start.1 = (f32[4,7,256,128]{3,2,1,0:T(8,128)S(1)}, f32[4,7,256,128]{3,2,1,0:T(8,128)}, u32[]{:S(2)}) copy-start(f32[4,7,256,128]{3,2,1,0:T(8,128)} %get-tuple-element.253) | copy-start | bytes 11010052 | tf_op jit(solution)/shard_map/while
  383.0 1.9 copy-start.2
  394.4 8.4 %copy-start.1 = (f32[4,7,256,128]{3,2,1,0:T(8,128)S(1)}, f32[4,7,256,128]{3,2,1,0:T(8,128)}, u32[]{:S(2)}) copy-start(f32[4,7,256,128]{3,2,1,0:T(8,128)} %get-tuple-element.253) | copy-start | bytes 11010052 | tf_op jit(solution)/shard_map/while
  410.8 1.9 copy-start.2
  422.1 8.4 %copy-start.1 = (f32[4,7,256,128]{3,2,1,0:T(8,128)S(1)}, f32[4,7,256,128]{3,2,1,0:T(8,128)}, u32[]{:S(2)}) copy-start(f32[4,7,256,128]{3,2,1,0:T(8,128)} %get-tuple-element.253) | copy-start | bytes 11010052 | tf_op jit(solution)/shard_map/while
  438.5 1.9 copy-start.2
  449.9 8.4 %copy-start.1 = (f32[4,7,256,128]{3,2,1,0:T(8,128)S(1)}, f32[4,7,256,128]{3,2,1,0:T(8,128)}, u32[]{:S(2)}) copy-start(f32[4,7,256,128]{3,2,1,0:T(8,128)} %get-tuple-element.253) | copy-start | bytes 11010052 | tf_op jit(solution)/shard_map/while
  466.3 1.9 copy-start.2
  477.6 8.4 %copy-start.1 = (f32[4,7,256,128]{3,2,1,0:T(8,128)S(1)}, f32[4,7,256,128]{3,2,1,0:T(8,128)}, u32[]{:S(2)}) copy-start(f32[4,7,256,128]{3,2,1,0:T(8,128)} %get-tuple-element.253) | copy-start | bytes 11010052 | tf_op jit(solution)/shard_map/while
  494.0 1.9 copy-start.2
  505.4 8.4 %copy-start.1 = (f32[4,7,256,128]{3,2,1,0:T(8,128)S(1)}, f32[4,7,256,128]{3,2,1,0:T(8,128)}, u32[]{:S(2)}) copy-start(f32[4,7,256,128]{3,2,1,0:T(8,128)} %get-tuple-element.253) | copy-start | bytes 11010052 | tf_op jit(solution)/shard_map/while
  521.8 1.9 copy-start.2
  533.1 8.4 %copy-start.1 = (f32[4,7,256,128]{3,2,1,0:T(8,128)S(1)}, f32[4,7,256,128]{3,2,1,0:T(8,128)}, u32[]{:S(2)}) copy-start(f32[4,7,256,128]{3,2,1,0:T(8,128)} %get-tuple-element.253) | copy-start | bytes 11010052 | tf_op jit(solution)/shard_map/while
  549.5 1.9 copy-start.2
  560.9 8.4 %copy-start.1 = (f32[4,7,256,128]{3,2,1,0:T(8,128)S(1)}, f32[4,7,256,128]{3,2,1,0:T(8,128)}, u32[]{:S(2)}) copy-start(f32[4,7,256,128]{3,2,1,0:T(8,128)} %get-tuple-element.253) | copy-start | bytes 11010052 | tf_op jit(solution)/shard_map/while
  577.3 1.9 copy-start.2
Sparse Core Ops, SparseCore 0:
  9.7 28.2 all-gather.8
  40.7 175.8 all-gather.4
  274.6 75.0 all-gather.6
where the time goes:
time: 597 us; the launch traced here: 595 us
  waiting for transfers between devices  297 us (50%)
  matrix products  131 us (22%)
  other arithmetic  87.5 us (15%)
  local copies, waits for them, and re-layouts  59.6 us (10%)
  between operations  13.9 us (2%)
    all_gather x1, waiting for transfers between devices, project_joined(): grouped = lax.all_gather(normed, 'gy', axis=0, tiled=True)  172 us
    reduce_sum x8, other arithmetic, attend(): total = total * shrink + jnp.sum(weights, axis=3)  66.5 us
    all_gather x1, waiting for transfers between devices, on_device(): piece = lax.all_gather(kv_rows, 'gy', axis=0, tiled=True)  65.9 us
    dot_general x8, matrix products, attend(): jnp.einsum('ghrn,ngo->ghro', weights.astype(jnp.bfloat16), value_part, pr...  64.3 us
    dot_general x8, matrix products, attend(): jnp.einsum('rgho,ngo->ghrn', queries, key_part, preferred_element_type=jn...  52.3 us
    all_to_all x1, waiting for transfers between devices, project_joined(): lax.all_to_all(block_out, 'gy', split_axis=0, concat_axis=1, tiled=True)  34.4 us
    all_gather x1, waiting for transfers between devices, project_joined(): lax.all_gather(weight, 'gx', axis=0, tiled=True)  24 us
    while x40, local copies, waits for them, and re-layouts  15 us
  transfers between devices with their start and end apart: 4, of which 4 were waited for; matrix products, arithmetic and copies ran while one was open for 4% of the time, Pallas kernels for 0%

commit v1 on v0

--- a/solution.py
+++ b/solution.py
@@ -37,7 +37,19 @@
 
 
 def project_joined(normed, weight, bias):
-    grouped = lax.all_gather(normed, "gy", axis=0, tiled=True)
+
+    def _enter_digits(body, named_axis):
+        return jnp.concatenate(
+            jax.lax.all_to_all(
+                jnp.stack([body for _ in range(jax.lax.axis_size(named_axis))], axis=0),
+                axis_name=named_axis,
+                split_axis=0,
+                concat_axis=0,
+            ),
+            axis=0,
+        )
+
+    grouped = _enter_digits(normed, "gy")
     summed = jnp.dot(
         grouped,
         lax.all_gather(weight, "gx", axis=0, tiled=True),

time: 597 us -> 845 us (1.42)
  waiting for transfers between devices: 297 us -> 531 us
  local copies, waits for them, and re-layouts: 59.6 us -> 69.7 us
    all_to_all x0 -> x1, waiting for transfers between devices: none -> 402 us  [_enter_digits(): jax.lax.all_to_all(jnp.stack([body for _ in range(jax.lax.axis_size(named...]
    all_gather x1 -> x0, waiting for transfers between devices: 172 us -> none  [project_joined(): grouped = lax.all_gather(normed, 'gy', axis=0, tiled=True)]
    another operation x0 -> x1, local copies, waits for them, and re-layouts: none -> 10.1 us  [_enter_digits(): jnp.stack([body for _ in range(jax.lax.axis_size(named_axis))], axis=0)]
  transfers between devices with their start and end apart: 4 -> 4, of which waited for: 4 -> 4; matrix products, arithmetic and copies ran while one was open for 4% -> 2% of each run, Pallas kernels for 0% -> 0%
where the time goes in v1:
time: 845 us; the launch traced here: 844 us
  waiting for transfers between devices  531 us (63%)
  matrix products  132 us (16%)
  other arithmetic  86.2 us (10%)
  local copies, waits for them, and re-layouts  69.7 us (8%)
  between operations  14.2 us (2%)
  starting transfers between devices  11.2 us (1%)
    all_to_all x1, waiting for transfers between devices, _enter_digits(): jax.lax.all_to_all(jnp.stack([body for _ in range(jax.lax.axis_size(named...  402 us
    all_gather x1, waiting for transfers between devices, on_device(): piece = lax.all_gather(kv_rows, 'gy', axis=0, tiled=True)  66.5 us
    reduce_sum x8, other arithmetic, attend(): total = total * shrink + jnp.sum(weights, axis=3)  66.5 us
    dot_general x8, matrix products, attend(): jnp.einsum('ghrn,ngo->ghro', weights.astype(jnp.bfloat16), value_part, pr...  64.3 us
    dot_general x8, matrix products, attend(): jnp.einsum('rgho,ngo->ghrn', queries, key_part, preferred_element_type=jn...  52.7 us
    all_to_all x1, waiting for transfers between devices, project_joined(): lax.all_to_all(block_out, 'gy', split_axis=0, concat_axis=1, tiled=True)  32.5 us
    all_gather x1, waiting for transfers between devices, project_joined(): lax.all_gather(weight, 'gx', axis=0, tiled=True)  29.3 us
  transfers between devices with their start and end apart: 4, of which 4 were waited for; matrix products, arithmetic and copies ran while one was open for 2% of the time, Pallas kernels for 0%

profile of v1, /device:TPU:0, one launch (start us, length us, event | category | flops | bytes accessed | tf_op | source)
XLA Modules:
  0.0 844.1 jit_solution(1912717674778952443)
XLA Ops:
  11.1 10.1 %stack.2 = bf16[16,256,3584]{2,1,0:T(8,128)(2,1)} broadcast(bf16[256,3584]{1,0:T(8,128)(2,1)S(1)} %fusion.19), dimensions={1,2} | broadcast | bytes 31195136 | tf_op jit(solution)/shard_map/stack | solution.py:44
  21.2 7.2 all-to-all-start
  29.9 29.3 %all-gather.6.cloned.1.call-done = bf16[8,448,288]{1,2,0:T(8,128)(2,1)} async-done(((bf16[1,448,288]{1,2,0:T(8,128)(2,1)}), bf16[8,448,288]{1,2,0:T(8,128)(2,1)}) %all-gather.6.cloned.1.call-update) | async-done | bytes 2064400 | tf_op jit(solution)/shard_map/all_gather | solution.py:55
  65.8 401.6 %all-to-all-done = bf16[16,256,3584]{2,1,0:T(8,128)(2,1)} async-done(((bf16[16,256,3584]{2,1,0:T(8,128)(2,1)}), bf16[16,256,3584]{2,1,0:T(8,128)(2,1)}, u32[]{:S(2)}, u32[]{:S(2)}) %all-to-all-start) | async-done | bytes 29360160 | tf_op jit(solution)/shard_map/all_to_all | solution.py:43
  467.4 14.7 %fusion.16 = bf16[4096,288]{0,1:T(8,128)(2,1)S(1)} fusion(bf16[4096,3584]{1,0:T(8,128)(2,1)} %bitcast.2, bf16[3584,288]{0,1:T(8,128)(2,1)} %reshape.178, f32[288]{0:T(512)S(1)} %dynamic_slice.11), kind=kOutput, calls=%fused_computation.25 | convolution fusion | flops 8458076160 | bytes 33784960 | tf_op jit(solution)/shard_map/dot_general | solution.py:53
  488.3 32.5 %all-to-all-done.1 = bf16[16,256,288]{1,2,0:T(8,128)(2,1)S(1)} async-done(((bf16[16,256,288]{1,2,0:T(8,128)(2,1)}), bf16[16,256,288]{1,2,0:T(8,128)(2,1)S(1)}, u32[]{:S(2)}, u32[]{:S(2)}) %all-to-all-start.1) | async-done | bytes 2359328 | tf_op jit(solution)/shard_map/all_to_all | solution.py:61
  531.2 66.5 %all-gather.4.cloned.1.call-done = bf16[4096,1024]{0,1:T(8,128)(2,1)} async-done(((bf16[256,1024]{0,1:T(8,128)(2,1)}), bf16[4096,1024]{0,1:T(8,128)(2,1)}) %all-gather.4.cloned.1.call-update) | async-done | bytes 8388624 | tf_op jit(solution)/shard_map/all_gather | solution.py:118
  597.7 7.5 copy.52
  605.2 222.4 %while.15 = (s32[]{:T(128)}, f32[4,7,256]{2,1,0:T(8,128)S(1)}, f32[4,7,256]{2,1,0:T(8,128)S(1)}, f32[4,7,256,128]{3,2,1,0:T(8,128)}, s32[256]{0:T(256)S(1)}, /*i...) while((s32[]{:T(128)}, f32[4,7,256]{2,1,0:T(8,128)S(1)}, ...), condition=%wide.region_8.9_spmd.clone, body=%wide.region_4.8_spmd.clone.sunk | while | flops 1922606336 | bytes 88814816 | solution.py:127
  608.1 6.6 fusion.43
  614.7 8.3 fusion.44
  623.0 8.0 fusion.46
  635.9 6.6 fusion.43
  642.5 8.3 fusion.44
  650.9 8.0 fusion.46
  663.7 6.6 fusion.43
  670.3 8.3 fusion.44
  678.6 8.0 fusion.46
  691.5 6.6 fusion.43
  698.1 8.3 fusion.44
  706.4 8.0 fusion.46
  725.9 8.3 fusion.44
  734.2 8.0 fusion.46
  747.1 6.6 fusion.43
  753.7 8.3 fusion.44
  762.0 8.0 fusion.46
  774.9 6.6 fusion.43
  781.5 8.3 fusion.44
  789.8 8.0 fusion.46
  802.7 6.6 fusion.43
  809.3 8.3 fusion.44
  817.6 8.0 fusion.46
  (153 shorter events, 83.2 us)
Async XLA Ops:
  21.2 446.2 %all-to-all-start = ((bf16[16,256,3584]{2,1,0:T(8,128)(2,1)}), bf16[16,256,3584]{2,1,0:T(8,128)(2,1)}, u32[]{:S(2)}, u32[]{:S(2)}) async-start(bf16[16,256,3584]{2,1,0:T(8,128)(2,1)} %stack.2), calls=%async_computation | async-start | bytes 58720256 | tf_op jit(solution)/shard_map/all_to_all | solution.py:43
  28.4 30.8 %all-gather.6.cloned.1.call-start = ((), (), s32[]{:S(2)}) async-start(), calls=%async_computation.3 | async-start | bytes 2654208 | tf_op jit(solution)/shard_map/all_gather | solution.py:55
  482.1 5.6 copy-start.3
  483.7 37.1 %all-to-all-start.1 = ((bf16[16,256,288]{1,2,0:T(8,128)(2,1)}), bf16[16,256,288]{1,2,0:T(8,128)(2,1)S(1)}, u32[]{:S(2)}, u32[]{:S(2)}) async-start(bf16[16,256,288]{1,2,0:T(8,128)(2,1)} %bitcast.86), calls=%async_computation.1 | async-start | bytes 4718592 | tf_op jit(solution)/shard_map/all_to_all | solution.py:61
  487.5 110.2 %all-gather.4.cloned.1.call-start = ((), (), s32[]{:S(2)}) async-start(), calls=%async_computation.2 | async-start | bytes 8912896 | tf_op jit(solution)/shard_map/all_gather | solution.py:118
  521.9 1.4 copy-start
  614.7 8.4 copy-start.1
  631.1 1.9 copy-start.2
  642.5 8.4 copy-start.1
  658.9 1.9 copy-start.2
  670.3 8.4 copy-start.1
  686.7 1.9 copy-start.2
  698.1 8.4 copy-start.1
  714.5 1.9 copy-start.2
  725.9 8.4 copy-start.1
  742.3 1.9 copy-start.2
  753.7 8.4 copy-start.1
  770.1 1.9 copy-start.2
  781.5 8.4 copy-start.1
  797.9 1.9 copy-start.2
  809.3 8.4 copy-start.1
  825.7 1.9 copy-start.2
Sparse Core Ops, SparseCore 0:
  30.9 28.3 all-gather.5
  522.1 75.5 all-gather.3
